TPU v7x, 256 devices: a whole 4x4x8 slice. The times are simulated.
256 devices in a mesh: seq: 64 (over z, x, core), head: 4 (over y).
Axes of the slice: x: 4, y: 4, z: 8, core: 2. Of those that a mesh axis runs over, the one named last changes fastest.
Arguments:
- features: bfloat16 [8192, 4096], P('seq', 'head'), may hold values from -6 to 6
- proj_weight: bfloat16 [4096, 4096], P(None, 'head'), may hold values from -0.09375 to 0.09375
- query_vectors: bfloat16 [8192, 4096], P('seq', 'head'), may hold values from -6 to 6
- key_vectors: bfloat16 [8192, 4096], P('seq', 'head'), may hold values from -6 to 6
Outputs:
- rotated_queries: bfloat16 [8192, 4096], P('seq', 'head')
- rotated_keys: bfloat16 [8192, 4096], P('seq', 'head')
All inputs are finite; a program needn't handle non-finite values.
Results may differ from a plain program's by a relative error of at most 0.0024.
Values may be sent and summed in bfloat16 or wider, within the bound.
No kernel may reach another device: no remote copies, remote signals or barrier semaphores. Data moves between devices by JAX's collectives and lax.ppermute only.
A program may use at most 128 MiB of HBM per device.

v0:
```python
import functools
import jax
import jax.numpy as jnp
from jax import lax
from jax.sharding import PartitionSpec as P

HEAD_DIM = 128


def entering(array, axis, count, combine, identity):
    place = lax.axis_index(axis)
    start = jnp.broadcast_to(jnp.asarray(identity, array.dtype), array.shape)
    span = array
    before = None
    shift = 1
    while shift < count:
        pairs = [(k, k + shift) for k in range(count - shift)]
        arrived = lax.ppermute(span, axis, pairs)
        reached = place >= shift
        last = shift * 2 >= count
        if before is None:
            before = jnp.where(reached, arrived, start)
            if not last:
                span = jnp.where(reached, combine(arrived, span), span)
        elif last:
            before = jnp.where(reached, combine(arrived, before), before)
        else:
            width = array.shape[-1]
            both = combine(arrived, jnp.concatenate([span, before], axis=-1))
            span = jnp.where(reached, both[..., :width], span)
            before = jnp.where(reached, both[..., width:], before)
        shift = shift * 2
    return before if before is not None else start


def small_inverse(matrix):
    highest = lax.Precision.HIGHEST
    size = matrix.shape[-1]
    position = jnp.arange(size)
    strict = (position[:, None] < position[None, :]).astype(jnp.float32)
    eye_block = jnp.eye(size, dtype=jnp.float32)
    power = -2.0 * matrix * strict[None]
    result = eye_block[None] + power
    reach = 2
    while reach < size:
        power = jnp.einsum("hij,hjk->hik", power, power, precision=highest)
        result = result + jnp.einsum("hij,hjk->hik", result, power, precision=highest)
        reach = reach * 2
    return 2.0 * result


def triangle_inverse(matrix):
    highest = lax.Precision.HIGHEST
    size = matrix.shape[-1]
    if size <= 16:
        return small_inverse(matrix)
    half = size // 2
    first = triangle_inverse(matrix[:, :half, :half])
    second = triangle_inverse(matrix[:, half:, half:])
    coupling = matrix[:, :half, half:]
    middle = jnp.einsum("hij,hjk->hik", first, coupling, precision=highest)
    corner = -jnp.einsum("hij,hjk->hik", middle, second, precision=highest)
    lower_left = jnp.zeros((matrix.shape[0], size - half, half), jnp.float32)
    top = jnp.concatenate([first, corner], axis=2)
    bottom = jnp.concatenate([lower_left, second], axis=2)
    return jnp.concatenate([top, bottom], axis=1)


def upper_solve(matrix, right_side):
    highest = lax.Precision.HIGHEST
    rows = matrix.shape[1]
    size = min(128, rows)
    count = rows // size
    solved_blocks = []
    for i in reversed(range(count)):
        inverse_block = triangle_inverse(matrix)
        solved_blocks.append(
            jnp.einsum("hij,hjk->hik", inverse_block, right_side, precision=highest)
        )
    return jnp.concatenate(solved_blocks[::-1], axis=1)


def body(seq_count, features, proj_weight, query_vectors, key_vectors):
    highest = lax.Precision.HIGHEST
    tok_rows = query_vectors.shape[0]
    width = proj_weight.shape[1]
    local_heads = width // HEAD_DIM
    raw_proj = jnp.dot(
        lax.all_gather(features, "head", axis=1, tiled=True),
        proj_weight,
        preferred_element_type=jnp.float32,
    )
    raw_proj = raw_proj.reshape(tok_rows, local_heads, HEAD_DIM)
    directions = raw_proj * lax.rsqrt(jnp.sum(raw_proj * raw_proj, axis=-1, keepdims=True) + 1e-06)
    reflectors = jnp.transpose(directions, (1, 0, 2))
    targets = jnp.concatenate(
        [
            query_vectors.reshape(tok_rows, local_heads, HEAD_DIM),
            key_vectors.reshape(tok_rows, local_heads, HEAD_DIM),
        ],
        axis=0,
    )
    targets = jnp.transpose(targets.astype(jnp.float32), (1, 0, 2))
    gram = jnp.einsum("hid,hjd->hij", reflectors, reflectors, precision=highest)
    position = jnp.arange(tok_rows)
    upper = (position[:, None] < position[None, :]).astype(jnp.float32)
    identity_tok = jnp.eye(tok_rows, dtype=jnp.float32)
    inverse_t = gram * upper[None] + 0.5 * identity_tok[None]
    projected = jnp.einsum("hid,htd->hit", reflectors, targets, precision=highest)
    target_pos = jnp.concatenate([position, position])
    keep = (position[:, None] <= target_pos[None, :]).astype(jnp.float32)
    masked = projected * keep[None]
    right_side = jnp.concatenate([masked, reflectors], axis=2)
    solved = upper_solve(inverse_t, right_side)
    weights_tok = solved[:, :, : 2 * tok_rows]
    factor = solved[:, :, 2 * tok_rows :]
    local_part = targets - jnp.einsum("hit,hid->htd", weights_tok, reflectors, precision=highest)
    identity = jnp.broadcast_to(
        jnp.eye(HEAD_DIM, dtype=jnp.float32), (local_heads, HEAD_DIM, HEAD_DIM)
    )
    block_product = identity - jnp.einsum("hid,hie->hde", reflectors, factor, precision=highest)

    def combine(earlier, later):
        return jnp.einsum("hde,hef->hdf", earlier, later, precision=highest)

    carried = entering(block_product, "seq", seq_count, combine, identity)
    rotated = jnp.einsum("hde,hte->htd", carried, local_part, precision=highest)
    rotated = jnp.transpose(rotated, (1, 0, 2))
    rotated_queries = rotated[:tok_rows].reshape(tok_rows, width).astype(jnp.bfloat16)
    rotated_keys = rotated[tok_rows:].reshape(tok_rows, width).astype(jnp.bfloat16)
    return (rotated_queries, rotated_keys)


def solution(mesh):
    in_specs = (P("seq", "head"), P(None, "head"), P("seq", "head"), P("seq", "head"))
    out_specs = (P("seq", "head"), P("seq", "head"))
    return jax.shard_map(
        functools.partial(body, mesh.shape["seq"]),
        mesh=mesh,
        in_specs=in_specs,
        out_specs=out_specs,
        check_vma=False,
    )
```

profile of v0, /device:TPU:35, one launch (start us, length us, event | category | flops | bytes accessed | tf_op | source)
XLA Modules:
  0.0 207.6 jit_solution(11913831428166195170)
XLA Ops:
  7.2 0.7 all-gather.2.cloned.1.call-update
  7.9 1.1 copy.86
  9.2 1.1 copy.85
  10.8 26.2 %all-gather.2.cloned.1.call-done = bf16[128,4096]{1,0:T(8,128)(2,1)} async-done(((bf16[128,1024]{1,0:T(8,128)(2,1)}), bf16[128,4096]{1,0:T(8,128)(2,1)}) %all-gather.2.cloned.1.call-update) | async-done | bytes 1048592 | tf_op jit(solution)/shard_map/all_gather | solution.py:89
  37.0 5.0 %fusion.141 = f32[128,1024]{1,0:T(8,128)S(1)} fusion(bf16[128,4096]{1,0:T(8,128)(2,1)} %all-gather.2.cloned.1.call-done, bf16[4096,1024]{1,0:T(8,128)(2,1)} %param.5), kind=kOutput, calls=%fused_computation.212 | convolution fusion | flops 1073741824 | bytes 9961472 | tf_op jit(solution)/shard_map/dot_general | solution.py:88
  42.1 0.2 multiply_reduce_fusion
  42.3 0.2 fusion.31
  42.6 1.2 fusion.5
  43.8 0.3 fusion.102
  44.1 0.3 fusion.101
  44.5 0.3 convolution_add_fusion.2
  44.8 0.3 convolution_add_fusion.5
  45.3 0.3 fusion.100
  45.6 0.3 convolution_add_fusion.8
  46.0 0.3 fusion.99
  46.3 0.3 convolution_add_fusion.11
  46.8 0.3 fusion.98
  47.0 0.3 convolution_add_fusion.14
  47.5 0.3 fusion.97
  47.8 0.3 convolution_add_fusion.17
  48.2 0.3 fusion.96
  48.5 0.3 convolution_add_fusion.20
  49.2 0.2 convolution_add_fusion.23
  50.5 0.3 fusion.76
  52.3 0.3 fusion.78
  52.8 0.2 convolution_negate_fusion.4
  53.0 0.3 fusion.61
  53.3 0.3 convolution_negate_fusion.1
  54.7 0.3 fusion.80
  56.3 0.2 fusion.143
  56.8 0.3 fusion.82
  57.3 0.3 fusion.63
  57.6 0.3 convolution_negate_fusion.2
  57.9 0.5 fusion.47
  58.4 0.4 convolution_negate_fusion
  58.8 0.6 convolution_multiply_fusion
  59.5 1.7 fusion
  61.2 1.0 convolution_subtract_fusion.1
  62.2 5.7 %collective-permute-start = (f32[8,128,128]{1,2,0:T(8,128)S(1)}, f32[8,128,128]{1,2,0:T(8,128)S(1)}, u32[]{:S(2)}, u32[]{:S(2)}) collective-permute-start(f32[8,128,128]{1,2,0:T(8,128)S(1)} %convolution_subtract_fusion.1), channel_id=1, source_target_pairs={{0,4},{4,8},{8,12},{12,16},{16,20},{20,24},{24,28},{28,32},{32,36}... | collective-permute-start | bytes 1572872 | tf_op jit(solution)/shard_map/ppermute | solution.py:18
  68.0 6.1 %collective-permute-done = f32[8,128,128]{1,2,0:T(8,128)S(1)} collective-permute-done((f32[8,128,128]{1,2,0:T(8,128)S(1)}, f32[8,128,128]{1,2,0:T(8,128)S(1)}, u32[]{:S(2)}, u32[]{:S(2)}) %collective-permute-start) | collective-permute-done | bytes 524320 | tf_op jit(solution)/shard_map/ppermute | solution.py:18
  74.1 1.8 convolution_select_fusion.1
  75.9 2.8 %collective-permute-start.1 = (f32[8,128,128]{1,2,0:T(8,128)S(1)}, f32[8,128,128]{1,2,0:T(8,128)}, u32[]{:S(2)}, u32[]{:S(2)}) collective-permute-start(f32[8,128,128]{1,2,0:T(8,128)S(1)} %convolution_select_fusion.1), channel_id=1, source_target_pairs={{0,8},{4,12},{8,16},{12,20},{16,24},{20,28},{24,32},{28,36},{32,40... | collective-permute-start | bytes 1572872 | tf_op jit(solution)/shard_map/ppermute | solution.py:18
  78.7 10.6 %collective-permute-done.1 = f32[8,128,128]{1,2,0:T(8,128)} collective-permute-done((f32[8,128,128]{1,2,0:T(8,128)S(1)}, f32[8,128,128]{1,2,0:T(8,128)}, u32[]{:S(2)}, u32[]{:S(2)}) %collective-permute-start.1) | collective-permute-done | bytes 524320 | tf_op jit(solution)/shard_map/ppermute | solution.py:18
  89.3 2.0 fusion.15
  91.3 1.1 slice_select_fusion.7
  92.5 4.6 %collective-permute-start.2 = (f32[8,128,128]{1,2,0:T(8,128)}, f32[8,128,128]{1,2,0:T(8,128)S(1)}, u32[]{:S(2)}, u32[]{:S(2)}) collective-permute-start(f32[8,128,128]{1,2,0:T(8,128)} %get-tuple-element.15), channel_id=1, source_target_pairs={{0,16},{4,20},{8,24},{12,28},{16,32},{20,36},{24,40},{28,44},{32,4... | collective-permute-start | bytes 1572872 | tf_op jit(solution)/shard_map/ppermute | solution.py:18
  97.1 10.6 %collective-permute-done.2 = f32[8,128,128]{1,2,0:T(8,128)S(1)} collective-permute-done((f32[8,128,128]{1,2,0:T(8,128)}, f32[8,128,128]{1,2,0:T(8,128)S(1)}, u32[]{:S(2)}, u32[]{:S(2)}) %collective-permute-start.2) | collective-permute-done | bytes 524320 | tf_op jit(solution)/shard_map/ppermute | solution.py:18
  107.7 2.2 %fusion.19 = f32[8,128,256]{1,2,0:T(8,128)S(1)} fusion(f32[8,128,128]{1,2,0:T(8,128)S(1)} %collective-permute-done.2, f32[8,128,128]{1,2,0:T(8,128)} %get-tuple-element.14, f32[8,128,128]{1,2,0:T(8,128)} %get-tuple-element.15), kind=kOutput, calls=%fused_computation.57 | convolution fusion | flops 402915328 | bytes 2621440 | tf_op jit(solution)/shard_map/hde,hef->hdf/dot_general | solution.py:124
  109.9 0.9 slice_select_fusion.5
  110.8 3.2 %collective-permute-start.3 = (f32[8,128,128]{1,2,0:T(8,128)}, f32[8,128,128]{1,2,0:T(8,128)S(1)}, u32[]{:S(2)}, u32[]{:S(2)}) collective-permute-start(f32[8,128,128]{1,2,0:T(8,128)} %get-tuple-element.13), channel_id=1, source_target_pairs={{0,32},{4,36},{8,40},{12,44},{16,48},{20,52},{24,56},{28,60},{32,6... | collective-permute-start | bytes 1572872 | tf_op jit(solution)/shard_map/ppermute | solution.py:18
  114.0 8.6 %collective-permute-done.3 = f32[8,128,128]{1,2,0:T(8,128)S(1)} collective-permute-done((f32[8,128,128]{1,2,0:T(8,128)}, f32[8,128,128]{1,2,0:T(8,128)S(1)}, u32[]{:S(2)}, u32[]{:S(2)}) %collective-permute-start.3) | collective-permute-done | bytes 524320 | tf_op jit(solution)/shard_map/ppermute | solution.py:18
  122.6 2.0 fusion.23
  124.8 9.3 %collective-permute-start.4 = (f32[8,128,128]{1,2,0:T(8,128)S(1)}, f32[8,128,128]{1,2,0:T(8,128)}, u32[]{:S(2)}, u32[]{:S(2)}) collective-permute-start(f32[8,128,128]{1,2,0:T(8,128)S(1)} %get-tuple-element.11), channel_id=1, source_target_pairs={{0,64},{4,68},{8,72},{12,76},{16,80},{20,84},{24,88},{28,92},{32,9... | collective-permute-start | bytes 1572872 | tf_op jit(solution)/shard_map/ppermute | solution.py:18
  134.1 32.4 %collective-permute-done.4 = f32[8,128,128]{1,2,0:T(8,128)} collective-permute-done((f32[8,128,128]{1,2,0:T(8,128)S(1)}, f32[8,128,128]{1,2,0:T(8,128)}, u32[]{:S(2)}, u32[]{:S(2)}) %collective-permute-start.4) | collective-permute-done | bytes 524320 | tf_op jit(solution)/shard_map/ppermute | solution.py:18
  166.6 2.0 fusion.27
  168.6 1.0 slice_select_fusion.2
  169.6 0.2 copy-done.2
  169.8 6.0 %collective-permute-start.5 = (f32[8,128,128]{1,2,0:T(8,128)}, f32[8,128,128]{1,2,0:T(8,128)S(1)}, u32[]{:S(2)}, u32[]{:S(2)}) collective-permute-start(f32[8,128,128]{1,2,0:T(8,128)} %slice_select_fusion.2), channel_id=1, source_target_pairs={{0,128},{4,132},{8,136},{12,140},{16,144},{20,148},{24,152},{28,15... | collective-permute-start | bytes 1572872 | tf_op jit(solution)/shard_map/ppermute | solution.py:18
  175.8 3.0 %convolution_subtract_fusion = f32[8,256,128]{2,1,0:T(8,128)S(1)} fusion(f32[8,128,128]{2,1,0:T(8,128)S(1)} %fusion.31, f32[8,128,384]{2,1,0:T(8,128)S(1)} %fusion, bf16[128,8,128]{2,0,1:T(8,128)(2,1)S(1)} %copy.88, bf16[128,8,128]{2,0,1:T(8,128)(2,1)} %copy-done.4), kind=kOutput, calls=%fused_computation.4 | convolution fusion | flops 404226048 | bytes 3145728 | tf_op jit(solution)/shard_map/hit,hid->htd/dot_general | solution.py:117
  178.8 18.4 %collective-permute-done.5 = f32[8,128,128]{1,2,0:T(8,128)S(1)} collective-permute-done((f32[8,128,128]{1,2,0:T(8,128)}, f32[8,128,128]{1,2,0:T(8,128)S(1)}, u32[]{:S(2)}, u32[]{:S(2)}) %collective-permute-start.5) | collective-permute-done | bytes 524320 | tf_op jit(solution)/shard_map/ppermute | solution.py:18
  197.2 0.6 convolution_select_fusion
  197.8 1.1 fusion.4
  199.0 0.9 copy.115
  199.9 0.8 copy.116
  (70 shorter events, 8.1 us)
Async XLA Ops:
  7.2 29.8 %all-gather.2.cloned.1.call-start = ((), (), s32[]{:S(2)}) async-start(), calls=%async_computation | async-start | bytes 1310720 | tf_op jit(solution)/shard_map/all_gather | solution.py:89
  10.5 48.3 %copy-start.4 = (bf16[128,8,128]{2,0,1:T(8,128)(2,1)}, bf16[128,8,128]{2,0,1:T(8,128)(2,1)S(1)}, u32[]{:S(2)}) copy-start(bf16[128,8,128]{2,0,1:T(8,128)(2,1)S(1)} %copy.87) | copy-start | bytes 786436
  62.2 5.8 %copy-start.5 = (f32[8,128,128]{1,2,0:T(8,128)}, f32[8,128,128]{1,2,0:T(8,128)S(1)}, u32[]{:S(2)}) copy-start(f32[8,128,128]{1,2,0:T(8,128)S(1)} %convolution_subtract_fusion.1) | copy-start | bytes 1572868
  62.2 11.9 %collective-permute-start = (f32[8,128,128]{1,2,0:T(8,128)S(1)}, f32[8,128,128]{1,2,0:T(8,128)S(1)}, u32[]{:S(2)}, u32[]{:S(2)}) collective-permute-start(f32[8,128,128]{1,2,0:T(8,128)S(1)} %convolution_subtract_fusion.1), channel_id=1, source_target_pairs={{0,4},{4,8},{8,12},{12,16},{16,20},{20,24},{24,28},{28,32},{32,36}... | collective-permute-start | bytes 1572872 | tf_op jit(solution)/shard_map/ppermute | solution.py:18
  75.9 13.4 %collective-permute-start.1 = (f32[8,128,128]{1,2,0:T(8,128)S(1)}, f32[8,128,128]{1,2,0:T(8,128)}, u32[]{:S(2)}, u32[]{:S(2)}) collective-permute-start(f32[8,128,128]{1,2,0:T(8,128)S(1)} %convolution_select_fusion.1), channel_id=1, source_target_pairs={{0,8},{4,12},{8,16},{12,20},{16,24},{20,28},{24,32},{28,36},{32,40... | collective-permute-start | bytes 1572872 | tf_op jit(solution)/shard_map/ppermute | solution.py:18
  92.5 17.4 %copy-start = (f32[8,128,128]{1,2,0:T(8,128)S(1)}, f32[8,128,128]{1,2,0:T(8,128)}, u32[]{:S(2)}) copy-start(f32[8,128,128]{1,2,0:T(8,128)} %get-tuple-element.14) | copy-start | bytes 1572868
  92.5 15.2 %collective-permute-start.2 = (f32[8,128,128]{1,2,0:T(8,128)}, f32[8,128,128]{1,2,0:T(8,128)S(1)}, u32[]{:S(2)}, u32[]{:S(2)}) collective-permute-start(f32[8,128,128]{1,2,0:T(8,128)} %get-tuple-element.15), channel_id=1, source_target_pairs={{0,16},{4,20},{8,24},{12,28},{16,32},{20,36},{24,40},{28,44},{32,4... | collective-permute-start | bytes 1572872 | tf_op jit(solution)/shard_map/ppermute | solution.py:18
  110.8 11.8 %copy-start.1 = (f32[8,128,128]{1,2,0:T(8,128)}, f32[8,128,128]{1,2,0:T(8,128)S(1)}, u32[]{:S(2)}) copy-start(f32[8,128,128]{1,2,0:T(8,128)S(1)} %get-tuple-element.12) | copy-start | bytes 1572868
  110.8 11.8 %collective-permute-start.3 = (f32[8,128,128]{1,2,0:T(8,128)}, f32[8,128,128]{1,2,0:T(8,128)S(1)}, u32[]{:S(2)}, u32[]{:S(2)}) collective-permute-start(f32[8,128,128]{1,2,0:T(8,128)} %get-tuple-element.13), channel_id=1, source_target_pairs={{0,32},{4,36},{8,40},{12,44},{16,48},{20,52},{24,56},{28,60},{32,6... | collective-permute-start | bytes 1572872 | tf_op jit(solution)/shard_map/ppermute | solution.py:18
  124.8 41.8 %collective-permute-start.4 = (f32[8,128,128]{1,2,0:T(8,128)S(1)}, f32[8,128,128]{1,2,0:T(8,128)}, u32[]{:S(2)}, u32[]{:S(2)}) collective-permute-start(f32[8,128,128]{1,2,0:T(8,128)S(1)} %get-tuple-element.11), channel_id=1, source_target_pairs={{0,64},{4,68},{8,72},{12,76},{16,80},{20,84},{24,88},{28,92},{32,9... | collective-permute-start | bytes 1572872 | tf_op jit(solution)/shard_map/ppermute | solution.py:18
  168.6 1.2 copy-start.2
  169.8 27.4 %collective-permute-start.5 = (f32[8,128,128]{1,2,0:T(8,128)}, f32[8,128,128]{1,2,0:T(8,128)S(1)}, u32[]{:S(2)}, u32[]{:S(2)}) collective-permute-start(f32[8,128,128]{1,2,0:T(8,128)} %slice_select_fusion.2), channel_id=1, source_target_pairs={{0,128},{4,132},{8,136},{12,140},{16,144},{20,148},{24,152},{28,15... | collective-permute-start | bytes 1572872 | tf_op jit(solution)/shard_map/ppermute | solution.py:18
  175.8 21.4 %copy-start.3 = (f32[8,128,256]{1,2,0:T(8,128)S(1)}, f32[8,128,256]{1,2,0:T(8,128)}, u32[]{:S(2)}) copy-start(f32[8,128,256]{1,2,0:T(8,128)} %copy-done.2) | copy-start | bytes 3145732
Sparse Core Ops, SparseCore 0:
  9.8 27.1 all-gather.1
where the time goes:
time: 208 us
  waiting for transfers between devices  114 us (55%)
  matrix products  38.3 us (18%)
  starting transfers between devices  31.7 us (15%)
  between operations  14.8 us (7%)
  local copies, waits for them, and re-layouts  5.15 us (2%)
  other arithmetic  4.06 us (2%)
    ppermute x6, waiting for transfers between devices, entering(): arrived = lax.ppermute(span, axis, pairs)  86.6 us
    ppermute x6, starting transfers between devices, entering(): arrived = lax.ppermute(span, axis, pairs)  31.7 us
    all_gather x1, waiting for transfers between devices, body(): lax.all_gather(features, 'head', axis=1, tiled=True)  26.2 us
    dot_general x6, matrix products, combine(): return jnp.einsum('hde,hef->hdf', earlier, later, precision=highest)  10.7 us
    dot_general x24, matrix products, small_inverse(): power = jnp.einsum('hij,hjk->hik', power, power, precision=highest)  5.09 us
    dot_general x24, matrix products, small_inverse(): jnp.einsum('hij,hjk->hik', result, power, precision=highest)  5.05 us
    dot_general x1, matrix products, body(): jnp.dot(lax.all_gather(features, 'head', axis=1, tiled=True), proj_weight...  4.97 us
    unnamed x17, local copies, waits for them, and re-layouts  4.26 us
  transfers between devices with their start and end apart: 7, of which 7 were waited for; matrix products, arithmetic and copies ran while one was open for 3% of the time, Pallas kernels for 0%

commit v1 on v0

--- a/solution.py
+++ b/solution.py
@@ -5,6 +5,11 @@
 from jax.sharding import PartitionSpec as P
 
 HEAD_DIM = 128
+
+
+def gather_by_exchange(x, axis, dim):
+    copies = jnp.concatenate([x] * lax.axis_size(axis), axis=dim)
+    return lax.all_to_all(copies, axis, dim, dim, tiled=True)
 
 
 def entering(array, axis, count, combine, identity):
@@ -86,9 +91,7 @@
     width = proj_weight.shape[1]
     local_heads = width // HEAD_DIM
     raw_proj = jnp.dot(
-        lax.all_gather(features, "head", axis=1, tiled=True),
-        proj_weight,
-        preferred_element_type=jnp.float32,
+        gather_by_exchange(features, "head", 1), proj_weight, preferred_element_type=jnp.float32
     )
     raw_proj = raw_proj.reshape(tok_rows, local_heads, HEAD_DIM)
     directions = raw_proj * lax.rsqrt(jnp.sum(raw_proj * raw_proj, axis=-1, keepdims=True) + 1e-06)

time: 208 us -> 190 us (0.913)
  waiting for transfers between devices: 114 us -> 86.5 us
  local copies, waits for them, and re-layouts: 5.15 us -> 20 us
  between operations: 14.8 us -> 1.49 us
  starting transfers between devices: 31.7 us -> 38.1 us
    all_gather x1 -> x0, waiting for transfers between devices: 26.2 us -> none  [body(): lax.all_gather(features, 'head', axis=1, tiled=True)]
    dot_general x0 -> x1, local copies, waits for them, and re-layouts: none -> 11.6 us  [body(): jnp.dot(gather_by_exchange(features, 'head', 1), proj_weight, preferred_e...]
    all_to_all x0 -> x1, starting transfers between devices: none -> 4.18 us  [gather_by_exchange(): return lax.all_to_all(copies, axis, dim, dim, tiled=True)]
    all_to_all x0 -> x3, local copies, waits for them, and re-layouts: none -> 3.18 us  [gather_by_exchange(): return lax.all_to_all(copies, axis, dim, dim, tiled=True)]
    ppermute x6, starting transfers between devices: 31.7 us -> 33.9 us  [entering(): arrived = lax.ppermute(span, axis, pairs)]
    unnamed x17 -> x25, local copies, waits for them, and re-layouts: 4.26 us -> 3.41 us
  transfers between devices with their start and end apart: 7 -> 7, of which waited for: 7 -> 7; matrix products, arithmetic and copies ran while one was open for 3% -> 9% of each run, Pallas kernels for 0% -> 0%
where the time goes in v1:
time: 190 us; the launch traced here: 189 us
  waiting for transfers between devices  86.5 us (46%)
  matrix products  39 us (21%)
  starting transfers between devices  38.1 us (20%)
  local copies, waits for them, and re-layouts  20 us (11%)
  other arithmetic  4.36 us (2%)
    ppermute x6, waiting for transfers between devices, entering(): arrived = lax.ppermute(span, axis, pairs)  85.4 us
    ppermute x6, starting transfers between devices, entering(): arrived = lax.ppermute(span, axis, pairs)  33.9 us
    dot_general x1, local copies, waits for them, and re-layouts, body(): jnp.dot(gather_by_exchange(features, 'head', 1), proj_weight, preferred_e...  11.6 us
    dot_general x6, matrix products, combine(): return jnp.einsum('hde,hef->hdf', earlier, later, precision=highest)  10.7 us
    dot_general x1, matrix products, body(): jnp.dot(gather_by_exchange(features, 'head', 1), proj_weight, preferred_e...  5.72 us
    dot_general x24, matrix products, small_inverse(): power = jnp.einsum('hij,hjk->hik', power, power, precision=highest)  5.09 us
    dot_general x24, matrix products, small_inverse(): jnp.einsum('hij,hjk->hik', result, power, precision=highest)  5.04 us
    all_to_all x1, starting transfers between devices, gather_by_exchange(): return lax.all_to_all(copies, axis, dim, dim, tiled=True)  4.18 us
  transfers between devices with their start and end apart: 7, of which 7 were waited for; matrix products, arithmetic and copies ran while one was open for 9% of the time, Pallas kernels for 0%

profile of v1, /device:TPU:35, one launch (start us, length us, event | category | flops | bytes accessed | tf_op | source)
XLA Modules:
  0.0 189.4 jit_solution(6724615597620428745)
XLA Ops:
  0.6 1.1 copy.108
  1.8 1.4 copy.112
  3.2 4.2 %all-to-all-start = ((bf16[128,4,1024]{2,0,1:T(8,128)(2,1)}), bf16[128,4,1024]{2,0,1:T(8,128)(2,1)S(1)}, u32[]{:S(2)}, u32[]{:S(2)}) async-start(bf16[128,4,1024]{2,0,1:T(8,128)(2,1)} %copy.112), calls=%async_computation | async-start | bytes 2097152 | tf_op jit(solution)/shard_map/all_to_all | solution.py:12
  7.4 11.6 %copy.171 = bf16[1024,4096]{1,0:T(8,128)(2,1)} copy(bf16[1024,4096]{0,1:T(8,128)(2,1)} %bitcast.125) | data formatting | bytes 16777216 | tf_op jit(solution)/shard_map/dot_general | solution.py:93
  19.9 0.7 fusion.74
  20.6 1.0 all-to-all-done
  21.6 0.8 copy.113
  22.4 1.0 reshape.91
  23.4 5.7 %multiply_reduce_fusion = (f32[128,8]{0,1:T(8,128)S(1)}, f32[128,8,128]{0,2,1:T(8,128)S(1)}) fusion(bf16[128,4096,1]{1,0,2:T(8,128)(2,1)S(1)} %reshape.91, bf16[8,128,4096]{2,1,0:T(8,128)(2,1)} %bitcast.124), kind=kOutput, calls=%fused_computation.95 | convolution fusion | flops 1074002944 | bytes 9965568 | tf_op jit(solution)/shard_map/dot_general | solution.py:93
  29.2 1.0 copy.118
  30.2 1.0 fusion.5
  31.2 0.3 fusion.101
  31.5 0.3 fusion.100
  32.0 0.3 convolution_add_fusion.2
  32.3 0.3 convolution_add_fusion.5
  32.7 0.3 fusion.99
  33.0 0.3 convolution_add_fusion.8
  33.5 0.3 fusion.98
  33.8 0.3 convolution_add_fusion.11
  34.2 0.3 fusion.97
  34.5 0.3 convolution_add_fusion.14
  35.0 0.3 fusion.96
  35.3 0.3 convolution_add_fusion.17
  35.7 0.3 fusion.95
  36.0 0.3 convolution_add_fusion.20
  38.0 0.3 fusion.75
  39.7 0.3 fusion.77
  40.5 0.3 fusion.60
  40.8 0.3 convolution_negate_fusion.1
  42.2 0.3 fusion.79
  44.3 0.3 fusion.81
  44.8 0.3 fusion.62
  45.1 0.3 convolution_negate_fusion.2
  45.4 0.5 fusion.46
  45.9 0.4 convolution_negate_fusion
  46.3 0.6 convolution_multiply_fusion
  47.0 1.8 fusion
  48.8 1.0 convolution_subtract_fusion.1
  49.8 4.8 %collective-permute-start = (f32[8,128,128]{1,2,0:T(8,128)S(1)}, f32[8,128,128]{1,2,0:T(8,128)S(1)}, u32[]{:S(2)}, u32[]{:S(2)}) collective-permute-start(f32[8,128,128]{1,2,0:T(8,128)S(1)} %convolution_subtract_fusion.1), channel_id=1, source_target_pairs={{0,4},{4,8},{8,12},{12,16},{16,20},{20,24},{24,28},{28,32},{32,36}... | collective-permute-start | bytes 1572872 | tf_op jit(solution)/shard_map/ppermute | solution.py:23
  54.7 6.1 %collective-permute-done = f32[8,128,128]{1,2,0:T(8,128)S(1)} collective-permute-done((f32[8,128,128]{1,2,0:T(8,128)S(1)}, f32[8,128,128]{1,2,0:T(8,128)S(1)}, u32[]{:S(2)}, u32[]{:S(2)}) %collective-permute-start) | collective-permute-done | bytes 524320 | tf_op jit(solution)/shard_map/ppermute | solution.py:23
  60.7 1.8 convolution_select_fusion.1
  62.6 2.8 %collective-permute-start.1 = (f32[8,128,128]{1,2,0:T(8,128)S(1)}, f32[8,128,128]{1,2,0:T(8,128)}, u32[]{:S(2)}, u32[]{:S(2)}) collective-permute-start(f32[8,128,128]{1,2,0:T(8,128)S(1)} %convolution_select_fusion.1), channel_id=1, source_target_pairs={{0,8},{4,12},{8,16},{12,20},{16,24},{20,28},{24,32},{28,36},{32,40... | collective-permute-start | bytes 1572872 | tf_op jit(solution)/shard_map/ppermute | solution.py:23
  65.5 10.6 %collective-permute-done.1 = f32[8,128,128]{1,2,0:T(8,128)} collective-permute-done((f32[8,128,128]{1,2,0:T(8,128)S(1)}, f32[8,128,128]{1,2,0:T(8,128)}, u32[]{:S(2)}, u32[]{:S(2)}) %collective-permute-start.1) | collective-permute-done | bytes 524320 | tf_op jit(solution)/shard_map/ppermute | solution.py:23
  76.0 2.0 %fusion.15 = f32[8,128,256]{1,2,0:T(8,128)S(1)} fusion(f32[8,128,128]{1,2,0:T(8,128)} %collective-permute-done.1, f32[8,128,128]{1,2,0:T(8,128)S(1)} %broadcast_select_fusion, f32[8,128,128]{1,2,0:T(8,128)S(1)} %convolution_select_fusion.1), kind=kOutput, calls=%fused_computation.54 | convolution fusion | flops 402915328 | bytes 2621440 | tf_op jit(solution)/shard_map/hde,hef->hdf/dot_general | solution.py:127
  78.1 1.1 slice_select_fusion.7
  79.2 5.2 %collective-permute-start.2 = (f32[8,128,128]{1,2,0:T(8,128)}, f32[8,128,128]{1,2,0:T(8,128)S(1)}, u32[]{:S(2)}, u32[]{:S(2)}) collective-permute-start(f32[8,128,128]{1,2,0:T(8,128)} %get-tuple-element.15), channel_id=1, source_target_pairs={{0,16},{4,20},{8,24},{12,28},{16,32},{20,36},{24,40},{28,44},{32,4... | collective-permute-start | bytes 1572872 | tf_op jit(solution)/shard_map/ppermute | solution.py:23
  84.4 10.0 %collective-permute-done.2 = f32[8,128,128]{1,2,0:T(8,128)S(1)} collective-permute-done((f32[8,128,128]{1,2,0:T(8,128)}, f32[8,128,128]{1,2,0:T(8,128)S(1)}, u32[]{:S(2)}, u32[]{:S(2)}) %collective-permute-start.2) | collective-permute-done | bytes 524320 | tf_op jit(solution)/shard_map/ppermute | solution.py:23
  94.4 2.2 %fusion.19 = f32[8,128,256]{1,2,0:T(8,128)S(1)} fusion(f32[8,128,128]{1,2,0:T(8,128)S(1)} %collective-permute-done.2, f32[8,128,128]{1,2,0:T(8,128)} %get-tuple-element.14, f32[8,128,128]{1,2,0:T(8,128)} %get-tuple-element.15), kind=kOutput, calls=%fused_computation.58 | convolution fusion | flops 402915328 | bytes 2621440 | tf_op jit(solution)/shard_map/hde,hef->hdf/dot_general | solution.py:127
  96.6 0.9 slice_select_fusion.5
  97.6 3.6 %collective-permute-start.3 = (f32[8,128,128]{1,2,0:T(8,128)}, f32[8,128,128]{1,2,0:T(8,128)S(1)}, u32[]{:S(2)}, u32[]{:S(2)}) collective-permute-start(f32[8,128,128]{1,2,0:T(8,128)} %get-tuple-element.13), channel_id=1, source_target_pairs={{0,32},{4,36},{8,40},{12,44},{16,48},{20,52},{24,56},{28,60},{32,6... | collective-permute-start | bytes 1572872 | tf_op jit(solution)/shard_map/ppermute | solution.py:23
  101.1 8.3 %collective-permute-done.3 = f32[8,128,128]{1,2,0:T(8,128)S(1)} collective-permute-done((f32[8,128,128]{1,2,0:T(8,128)}, f32[8,128,128]{1,2,0:T(8,128)S(1)}, u32[]{:S(2)}, u32[]{:S(2)}) %collective-permute-start.3) | collective-permute-done | bytes 524320 | tf_op jit(solution)/shard_map/ppermute | solution.py:23
  109.4 2.0 %fusion.23 = f32[8,128,256]{1,2,0:T(8,128)S(1)} fusion(f32[8,128,128]{1,2,0:T(8,128)S(1)} %collective-permute-done.3, f32[8,128,128]{1,2,0:T(8,128)S(1)} %get-tuple-element.12, f32[8,128,128]{1,2,0:T(8,128)} %get-tuple-element.13), kind=kOutput, calls=%fused_computation.62 | convolution fusion | flops 402915328 | bytes 2621440 | tf_op jit(solution)/shard_map/hde,hef->hdf/dot_general | solution.py:127
  111.6 11.2 %collective-permute-start.4 = (f32[8,128,128]{1,2,0:T(8,128)S(1)}, f32[8,128,128]{1,2,0:T(8,128)}, u32[]{:S(2)}, u32[]{:S(2)}) collective-permute-start(f32[8,128,128]{1,2,0:T(8,128)S(1)} %get-tuple-element.11), channel_id=1, source_target_pairs={{0,64},{4,68},{8,72},{12,76},{16,80},{20,84},{24,88},{28,92},{32,9... | collective-permute-start | bytes 1572872 | tf_op jit(solution)/shard_map/ppermute | solution.py:23
  122.8 32.4 %collective-permute-done.4 = f32[8,128,128]{1,2,0:T(8,128)} collective-permute-done((f32[8,128,128]{1,2,0:T(8,128)S(1)}, f32[8,128,128]{1,2,0:T(8,128)}, u32[]{:S(2)}, u32[]{:S(2)}) %collective-permute-start.4) | collective-permute-done | bytes 524320 | tf_op jit(solution)/shard_map/ppermute | solution.py:23
  155.2 2.0 %fusion.27 = f32[8,128,256]{1,2,0:T(8,128)S(1)} fusion(f32[8,128,128]{1,2,0:T(8,128)} %collective-permute-done.4, f32[8,128,128]{1,2,0:T(8,128)S(1)} %get-tuple-element.10, f32[8,128,128]{1,2,0:T(8,128)S(1)} %get-tuple-element.11), kind=kOutput, calls=%fused_computation.66 | convolution fusion | flops 402915328 | bytes 2621440 | tf_op jit(solution)/shard_map/hde,hef->hdf/dot_general | solution.py:127
  157.3 1.0 slice_select_fusion.2
  158.2 0.2 copy-done.2
  158.4 6.4 %collective-permute-start.5 = (f32[8,128,128]{1,2,0:T(8,128)}, f32[8,128,128]{1,2,0:T(8,128)S(1)}, u32[]{:S(2)}, u32[]{:S(2)}) collective-permute-start(f32[8,128,128]{1,2,0:T(8,128)} %slice_select_fusion.2), channel_id=1, source_target_pairs={{0,128},{4,132},{8,136},{12,140},{16,144},{20,148},{24,152},{28,15... | collective-permute-start | bytes 1572872 | tf_op jit(solution)/shard_map/ppermute | solution.py:23
  164.8 3.0 %convolution_subtract_fusion = f32[8,256,128]{2,1,0:T(8,128)S(1)} fusion(f32[8,128,128]{1,2,0:T(8,128)S(1)} %bitcast_multiply_fusion, f32[8,128,384]{2,1,0:T(8,128)S(1)} %fusion, bf16[128,8,128]{2,0,1:T(8,128)(2,1)S(1)} %copy.107, bf16[128,8,128]{2,0,1:T(8,128)(2,1)} %copy-done.4), kind=kOutput, calls=%fused_computation.4 | convolution fusion | flops 404226048 | bytes 3145728 | tf_op jit(solution)/shard_map/hit,hid->htd/dot_general | solution.py:120
  167.8 18.0 %collective-permute-done.5 = f32[8,128,128]{1,2,0:T(8,128)S(1)} collective-permute-done((f32[8,128,128]{1,2,0:T(8,128)}, f32[8,128,128]{1,2,0:T(8,128)S(1)}, u32[]{:S(2)}, u32[]{:S(2)}) %collective-permute-start.5) | collective-permute-done | bytes 524320 | tf_op jit(solution)/shard_map/ppermute | solution.py:23
  185.8 0.6 convolution_select_fusion
  186.4 1.1 fusion.4
  187.7 0.9 copy.145
  188.5 0.8 copy.146
  (81 shorter events, 9.0 us)
Async XLA Ops:
  3.2 18.4 %all-to-all-start = ((bf16[128,4,1024]{2,0,1:T(8,128)(2,1)}), bf16[128,4,1024]{2,0,1:T(8,128)(2,1)S(1)}, u32[]{:S(2)}, u32[]{:S(2)}) async-start(bf16[128,4,1024]{2,0,1:T(8,128)(2,1)} %copy.112), calls=%async_computation | async-start | bytes 2097152 | tf_op jit(solution)/shard_map/all_to_all | solution.py:12
  7.4 11.6 %copy-start.8 = (bf16[128,1024]{1,0:T(8,128)(2,1)S(1)}, bf16[128,1024]{1,0:T(8,128)(2,1)}, u32[]{:S(2)}) copy-start(bf16[128,1024]{1,0:T(8,128)(2,1)} %param.7) | copy-start | bytes 786436
  7.4 11.9 %copy-start.9 = (bf16[128,1024]{1,0:T(8,128)(2,1)S(1)}, bf16[128,1024]{1,0:T(8,128)(2,1)}, u32[]{:S(2)}) copy-start(bf16[128,1024]{1,0:T(8,128)(2,1)} %param.6) | copy-start | bytes 786436
  19.7 26.6 %copy-start.4 = (bf16[128,8,128]{2,0,1:T(8,128)(2,1)}, bf16[128,8,128]{2,0,1:T(8,128)(2,1)S(1)}, u32[]{:S(2)}) copy-start(bf16[128,8,128]{2,0,1:T(8,128)(2,1)S(1)} %copy.106) | copy-start | bytes 786436
  43.2 3.1 %copy-start.7 = (f32[128,256]{1,0:T(8,128)S(1)}, f32[128,256]{1,0:T(8,128)}, u32[]{:S(2)}) copy-start(f32[128,256]{1,0:T(8,128)} %fusion.74) | copy-start | bytes 393220
  45.1 1.9 copy-start.6
  49.8 4.8 %copy-start.5 = (f32[8,128,128]{1,2,0:T(8,128)}, f32[8,128,128]{1,2,0:T(8,128)S(1)}, u32[]{:S(2)}) copy-start(f32[8,128,128]{1,2,0:T(8,128)S(1)} %convolution_subtract_fusion.1) | copy-start | bytes 1572868
  49.8 10.9 %collective-permute-start = (f32[8,128,128]{1,2,0:T(8,128)S(1)}, f32[8,128,128]{1,2,0:T(8,128)S(1)}, u32[]{:S(2)}, u32[]{:S(2)}) collective-permute-start(f32[8,128,128]{1,2,0:T(8,128)S(1)} %convolution_subtract_fusion.1), channel_id=1, source_target_pairs={{0,4},{4,8},{8,12},{12,16},{16,20},{20,24},{24,28},{28,32},{32,36}... | collective-permute-start | bytes 1572872 | tf_op jit(solution)/shard_map/ppermute | solution.py:23
  62.6 13.5 %collective-permute-start.1 = (f32[8,128,128]{1,2,0:T(8,128)S(1)}, f32[8,128,128]{1,2,0:T(8,128)}, u32[]{:S(2)}, u32[]{:S(2)}) collective-permute-start(f32[8,128,128]{1,2,0:T(8,128)S(1)} %convolution_select_fusion.1), channel_id=1, source_target_pairs={{0,8},{4,12},{8,16},{12,20},{16,24},{20,28},{24,32},{28,36},{32,40... | collective-permute-start | bytes 1572872 | tf_op jit(solution)/shard_map/ppermute | solution.py:23
  79.2 17.4 %copy-start = (f32[8,128,128]{1,2,0:T(8,128)S(1)}, f32[8,128,128]{1,2,0:T(8,128)}, u32[]{:S(2)}) copy-start(f32[8,128,128]{1,2,0:T(8,128)} %get-tuple-element.14) | copy-start | bytes 1572868
  79.2 15.2 %collective-permute-start.2 = (f32[8,128,128]{1,2,0:T(8,128)}, f32[8,128,128]{1,2,0:T(8,128)S(1)}, u32[]{:S(2)}, u32[]{:S(2)}) collective-permute-start(f32[8,128,128]{1,2,0:T(8,128)} %get-tuple-element.15), channel_id=1, source_target_pairs={{0,16},{4,20},{8,24},{12,28},{16,32},{20,36},{24,40},{28,44},{32,4... | collective-permute-start | bytes 1572872 | tf_op jit(solution)/shard_map/ppermute | solution.py:23
  97.6 11.8 %copy-start.1 = (f32[8,128,128]{1,2,0:T(8,128)}, f32[8,128,128]{1,2,0:T(8,128)S(1)}, u32[]{:S(2)}) copy-start(f32[8,128,128]{1,2,0:T(8,128)S(1)} %get-tuple-element.12) | copy-start | bytes 1572868
  97.6 11.8 %collective-permute-start.3 = (f32[8,128,128]{1,2,0:T(8,128)}, f32[8,128,128]{1,2,0:T(8,128)S(1)}, u32[]{:S(2)}, u32[]{:S(2)}) collective-permute-start(f32[8,128,128]{1,2,0:T(8,128)} %get-tuple-element.13), channel_id=1, source_target_pairs={{0,32},{4,36},{8,40},{12,44},{16,48},{20,52},{24,56},{28,60},{32,6... | collective-permute-start | bytes 1572872 | tf_op jit(solution)/shard_map/ppermute | solution.py:23
  111.6 43.6 %collective-permute-start.4 = (f32[8,128,128]{1,2,0:T(8,128)S(1)}, f32[8,128,128]{1,2,0:T(8,128)}, u32[]{:S(2)}, u32[]{:S(2)}) collective-permute-start(f32[8,128,128]{1,2,0:T(8,128)S(1)} %get-tuple-element.11), channel_id=1, source_target_pairs={{0,64},{4,68},{8,72},{12,76},{16,80},{20,84},{24,88},{28,92},{32,9... | collective-permute-start | bytes 1572872 | tf_op jit(solution)/shard_map/ppermute | solution.py:23
  157.2 1.2 copy-start.2
  158.4 27.4 %collective-permute-start.5 = (f32[8,128,128]{1,2,0:T(8,128)}, f32[8,128,128]{1,2,0:T(8,128)S(1)}, u32[]{:S(2)}, u32[]{:S(2)}) collective-permute-start(f32[8,128,128]{1,2,0:T(8,128)} %slice_select_fusion.2), channel_id=1, source_target_pairs={{0,128},{4,132},{8,136},{12,140},{16,144},{20,148},{24,152},{28,15... | collective-permute-start | bytes 1572872 | tf_op jit(solution)/shard_map/ppermute | solution.py:23
  164.8 21.0 %copy-start.3 = (f32[8,128,256]{1,2,0:T(8,128)S(1)}, f32[8,128,256]{1,2,0:T(8,128)}, u32[]{:S(2)}) copy-start(f32[8,128,256]{1,2,0:T(8,128)} %copy-done.2) | copy-start | bytes 3145732
